TPU v7x, 512 devices: a whole 4x4x16 slice. The times are simulated.
512 devices in a mesh: pole: 2 (over core), prow: 16 (over z), pcol: 16 (over x, y).
Axes of the slice: x: 4, y: 4, z: 16, core: 2. Of those that a mesh axis runs over, the one named last changes fastest.
Arguments:
- inverse_trailing: float32 [32768, 16384], P(('pole', 'prow'), 'pcol'), parts along dimension 0, may hold values from -6 to 6
- factor_blocks: float32 [6, 4096, 256], P('pole', 'prow'), parts along dimension 0, may hold values from -0.09375 to 0.09375
- diag_pivots: float32 [256, 6, 256], P('pcol', 'pole'), parts along dimension 1, may hold values from -6 to 6
- structure: int32 [3, 16], replicated, may hold values from 0 to 63, as said below
- owner_map: int32 [64], replicated, may hold values from 0 to 63, each once
Outputs:
- row_inverse: float32 [256, 6, 16384], P('pcol', 'pole', 'prow'), parts along dimension 1
- diag_inverse: float32 [256, 6, 256], P('pcol', 'pole'), parts along dimension 1
There are 2 independent parts, one for each index of `pole`. A program takes and returns all parts, laid end to end along the dimension named above; an argument that names none is the same for every part. Nothing has to cross between parts.
Inputs may be any that keep to these rules, and one draw needn't show every extreme that they name: `structure`: each row lists 16 distinct logical ancestor blocks.
All inputs are finite; a program needn't handle non-finite values.
Results may differ from a plain program's by a relative error of at most 0.0001.
Values sent between devices are 32-bit elements; how exact they have to be, the bound alone decides.
No kernel may reach another device: no remote copies, remote signals or barrier semaphores. Data moves between devices by JAX's collectives and lax.ppermute only.
A program may use at most 64 MiB of HBM per device.

v0:
```python
import jax
import jax.numpy as jnp
from jax import lax
from jax.sharding import PartitionSpec as P


def diag_product(values, factor):
    return jnp.einsum("awj,wjb->awb", values, factor, precision=lax.Precision.HIGHEST)


def shards(inverse_trailing, factor_blocks, diag_pivots, structure, owner_map):
    width = factor_blocks.shape[2]
    window = factor_blocks.shape[0]
    owned = inverse_trailing.shape[0] // width
    ancestors = owner_map.shape[0]
    row_index = lax.axis_index("prow")
    col_index = lax.axis_index("pcol")
    catalog = jnp.arange(ancestors, dtype=jnp.int32)
    positions = jnp.sum(
        jnp.where(structure[:, :, None] == catalog[None, None, :], owner_map[None, None, :], 0),
        axis=2,
    )
    slots = jnp.arange(owned, dtype=jnp.int32)
    col_slots = col_index * owned + slots
    row_slots = row_index * owned + slots
    piece = lax.all_gather(factor_blocks, "prow", axis=1, tiled=True)
    count = piece.shape[1] // width
    blocks = piece.reshape(window, count, width, width)
    col_pick = (positions[:, None, :] == col_slots[None, :, None]).astype(jnp.float32)
    row_pick = (positions[:, None, :] == row_slots[None, :, None]).astype(jnp.float32)
    col_acc = jnp.einsum("wsi,wiab->wsab", col_pick, blocks, precision=lax.Precision.HIGHEST)
    row_acc = jnp.einsum("wsi,wiab->wsab", row_pick, blocks, precision=lax.Precision.HIGHEST)
    col_factor = col_acc.reshape(window, owned * width, width)
    row_factor = row_acc.reshape(window, owned * width, width)
    in_rows = jnp.any(positions[:, None, :] == row_slots[None, :, None], axis=2).astype(jnp.float32)
    row_mask = jnp.repeat(in_rows, width, axis=1)
    summed = lax.psum_scatter(
        -jnp.einsum("wja,ij->awi", col_factor, inverse_trailing, precision=lax.Precision.HIGHEST),
        "pcol",
        scatter_dimension=0,
        tiled=True,
    )
    row_inverse = summed * row_mask[None, :, :]
    local_diag = diag_product(row_inverse, row_factor)
    total_diag = lax.psum(local_diag, "prow")
    diag_inverse = diag_pivots - total_diag
    return (row_inverse, diag_inverse)


def solution(mesh):
    in_specs = (
        P(("pole", "prow"), "pcol"),
        P("pole", "prow", None),
        P("pcol", "pole", None),
        P(),
        P(),
    )
    out_specs = (P("pcol", "pole", "prow"), P("pcol", "pole", None))
    return jax.shard_map(shards, mesh=mesh, in_specs=in_specs, out_specs=out_specs, check_vma=False)
```

profile of v0, /device:TPU:2, one launch (start us, length us, event | category | flops | bytes accessed | tf_op | source)
XLA Modules:
  0.0 359.3 jit_solution(15618497550631797289)
XLA Ops:
  7.2 0.0 all-gather.2.cloned.1.call-start
  7.2 0.7 all-gather.2.cloned.1.call-update
  7.9 0.0 reduce-scatter.2.cloned.1.call-start
  8.0 0.9 select_reduce_fusion
  8.9 153.8 %all-gather.2.cloned.1.call-done = f32[3,4096,256]{2,1,0:T(8,128)} async-done(((f32[3,256,256]{2,1,0:T(8,128)}), f32[3,4096,256]{2,1,0:T(8,128)}) %all-gather.2.cloned.1.call-update) | async-done | bytes 12582928 | tf_op jit(solution)/shard_map/all_gather | solution.py:26
  162.6 16.1 %fusion.2 = f32[3,4,256,256]{3,1,2,0:T(4,128)S(1)} fusion(f32[3,16,256,256]{3,2,1,0:T(8,128)} %bitcast.28, s32[3,16]{1,0:T(4,128)S(1)} %select_reduce_fusion, s32[4]{0:T(128)S(1)} %iota_add_fusion.1), kind=kOutput, calls=%fused_computation.2 | convolution fusion | flops 150995136 | bytes 15728848 | tf_op jit(solution)/shard_map/wsi,wiab->wsab/dot_general | solution.py:31
  178.8 0.0 copy-start
  178.8 0.5 copy.13
  179.3 1.6 copy-done
  181.0 22.3 %negate_bitcast_fusion = f32[256,3,1024]{2,0,1:T(8,128)} fusion(f32[3,1024,256]{2,1,0:T(8,128)S(1)} %bitcast.31, f32[1024,1024]{1,0:T(8,128)S(1)} %copy-done), kind=kOutput, calls=%fused_computation.6 | convolution fusion | flops 9664462848 | bytes 10485760 | tf_op jit(solution)/shard_map/wja,ij->awi/dot_general | solution.py:38
  203.3 0.0 reduce-scatter.2.cloned.1.call-update
  203.3 0.2 compare_reduce_fusion
  203.5 0.1 broadcast_bitcast_fusion
  203.6 15.8 %fusion = f32[3,4,256,256]{3,1,2,0:T(4,128)S(1)} fusion(f32[3,16,256,256]{3,2,1,0:T(8,128)} %bitcast.29, s32[3,16]{1,0:T(4,128)S(1)} %select_reduce_fusion, s32[4]{0:T(128)S(1)} %iota_add_fusion), kind=kOutput, calls=%fused_computation | convolution fusion | flops 150995136 | bytes 15728848 | tf_op jit(solution)/shard_map/wsi,wiab->wsab/dot_general | solution.py:32
  219.4 0.5 copy.16
  220.0 0.0 copy-start.2
  220.0 72.0 %reduce-scatter.2.cloned.1.call-done = f32[16,3,1024]{2,0,1:T(8,128)} async-done(((f32[256,3,1024]{2,0,1:T(8,128)}), f32[16,3,1024]{2,0,1:T(8,128)}) %reduce-scatter.2.cloned.1.call-update) | async-done | bytes 196624 | tf_op jit(solution)/shard_map/reduce_scatter | solution.py:37
  292.0 0.9 broadcast_multiply_fusion
  293.0 0.0 copy-start.1
  293.0 1.7 convolution_bitcast_fusion
  294.7 56.9 %psum.7 = f32[16,3,256]{2,0,1:T(8,128)S(1)} all-reduce(f32[16,3,256]{2,0,1:T(8,128)S(1)} %convolution_bitcast_fusion), channel_id=1, replica_groups=mesh['pole'=2,'prow'=16,'pcol'=16] {'prow'}, use_global_device_ids=true, to_apply=%region_3.4 | all-reduce | flops 12288 | bytes 98304 | tf_op jit(solution)/shard_map/psum | solution.py:45
  351.6 0.0 copy-done.2
  351.6 0.6 sub.3
  352.2 0.0 copy-done.1
  (4 shorter events, 0.0 us)
Async XLA Ops:
  7.2 155.5 %all-gather.2.cloned.1.call-start = ((), (), s32[]{:S(2)}) async-start(), calls=%async_computation.1 | async-start | bytes 13369344 | tf_op jit(solution)/shard_map/all_gather | solution.py:26
  7.9 284.1 %reduce-scatter.2.cloned.1.call-start = ((), (), s32[]{:S(2)}) async-start(), calls=%async_computation.2 | async-start | bytes 3342336 | tf_op jit(solution)/shard_map/reduce_scatter | solution.py:37
  178.8 2.2 copy-start
  220.0 131.6 %copy-start.2 = (f32[16,3,256]{2,0,1:T(8,128)S(1)}, f32[16,3,256]{2,0,1:T(8,128)}, u32[]{:S(2)}) copy-start(f32[16,3,256]{2,0,1:T(8,128)} %param.7) | copy-start | bytes 147460
  293.0 59.3 %copy-start.1 = (f32[16,3,1024]{2,0,1:T(8,128)}, f32[16,3,1024]{2,0,1:T(8,128)S(1)}, u32[]{:S(2)}) copy-start(f32[16,3,1024]{2,0,1:T(8,128)S(1)} %broadcast_multiply_fusion) | copy-start | bytes 589828
Sparse Core Ops, SparseCore 0:
  10.1 152.5 all-gather.1
  203.4 88.5 reduce-scatter.1
where the time goes:
time: 365 us; the launch traced here: 359 us
  waiting for transfers between devices  226 us (62%)
  blocking collectives  56.9 us (16%)
  matrix products  56 us (15%)
  between operations  14.4 us (4%)
    all_gather x1, waiting for transfers between devices, shards(): piece = lax.all_gather(factor_blocks, 'prow', axis=1, tiled=True)  154 us
    reduce_scatter x1, waiting for transfers between devices, shards(): lax.psum_scatter(-jnp.einsum('wja,ij->awi', col_factor, inverse_trailing,...  72 us
    psum x1, blocking collectives, shards(): total_diag = lax.psum(local_diag, 'prow')  56.9 us
    dot_general x1, matrix products, shards(): jnp.einsum('wja,ij->awi', col_factor, inverse_trailing, precision=lax.Pre...  22.3 us
    dot_general x1, matrix products, shards(): jnp.einsum('wsi,wiab->wsab', col_pick, blocks, precision=lax.Precision.HI...  16.1 us
    dot_general x1, matrix products, shards(): jnp.einsum('wsi,wiab->wsab', row_pick, blocks, precision=lax.Precision.HI...  15.8 us
  transfers between devices with their start and end apart: 2, of which 2 were waited for; matrix products, arithmetic and copies ran while one was open for 5% of the time, Pallas kernels for 0%

commit v1 on v0

--- a/solution.py
+++ b/solution.py
@@ -42,7 +42,7 @@
     )
     row_inverse = summed * row_mask[None, :, :]
     local_diag = diag_product(row_inverse, row_factor)
-    total_diag = lax.psum(local_diag, "prow")
+    total_diag = jax.lax.all_gather(local_diag, "prow").sum(axis=0)
     diag_inverse = diag_pivots - total_diag
     return (row_inverse, diag_inverse)
 

time: 365 us -> 343 us (0.940)
  blocking collectives: 56.9 us -> 34.8 us
    psum x1 -> x0, blocking collectives: 56.9 us -> none  [shards(): total_diag = lax.psum(local_diag, 'prow')]
    all_gather x0 -> x1, blocking collectives: none -> 34.8 us  [shards(): total_diag = jax.lax.all_gather(local_diag, 'prow').sum(axis=0)]
where the time goes in v1:
time: 343 us; the launch traced here: 337 us
  waiting for transfers between devices  226 us (66%)
  matrix products  56 us (16%)
  blocking collectives  34.8 us (10%)
  between operations  14.4 us (4%)
    all_gather x1, waiting for transfers between devices, shards(): piece = lax.all_gather(factor_blocks, 'prow', axis=1, tiled=True)  154 us
    reduce_scatter x1, waiting for transfers between devices, shards(): lax.psum_scatter(-jnp.einsum('wja,ij->awi', col_factor, inverse_trailing,...  72 us
    all_gather x1, blocking collectives, shards(): total_diag = jax.lax.all_gather(local_diag, 'prow').sum(axis=0)  34.8 us
    dot_general x1, matrix products, shards(): jnp.einsum('wja,ij->awi', col_factor, inverse_trailing, precision=lax.Pre...  22.3 us
    dot_general x1, matrix products, shards(): jnp.einsum('wsi,wiab->wsab', col_pick, blocks, precision=lax.Precision.HI...  16.1 us
    dot_general x1, matrix products, shards(): jnp.einsum('wsi,wiab->wsab', row_pick, blocks, precision=lax.Precision.HI...  15.8 us
  transfers between devices with their start and end apart: 2, of which 2 were waited for; matrix products, arithmetic and copies ran while one was open for 5% of the time, Pallas kernels for 0%

profile of v1, /device:TPU:2, one launch (start us, length us, event | category | flops | bytes accessed | tf_op | source)
XLA Modules:
  0.0 337.3 jit_solution(7485519224508859698)
XLA Ops:
  7.2 0.0 all-gather.3.cloned.1.call-start
  7.2 0.7 all-gather.3.cloned.1.call-update
  7.9 0.0 reduce-scatter.2.cloned.1.call-start
  8.0 0.9 select_reduce_fusion
  8.9 153.8 %all-gather.3.cloned.1.call-done = f32[3,4096,256]{2,1,0:T(8,128)} async-done(((f32[3,256,256]{2,1,0:T(8,128)}), f32[3,4096,256]{2,1,0:T(8,128)}) %all-gather.3.cloned.1.call-update) | async-done | bytes 12582928 | tf_op jit(solution)/shard_map/all_gather | solution.py:26
  162.6 16.1 %fusion.2 = f32[3,4,256,256]{3,1,2,0:T(4,128)S(1)} fusion(f32[3,16,256,256]{3,2,1,0:T(8,128)} %bitcast.29, s32[3,16]{1,0:T(4,128)S(1)} %select_reduce_fusion, s32[4]{0:T(128)S(1)} %iota_add_fusion.1), kind=kOutput, calls=%fused_computation.2 | convolution fusion | flops 150995136 | bytes 15728848 | tf_op jit(solution)/shard_map/wsi,wiab->wsab/dot_general | solution.py:31
  178.8 0.0 copy-start
  178.8 0.5 copy.13
  179.3 1.6 copy-done
  181.0 22.3 %negate_bitcast_fusion = f32[256,3,1024]{2,0,1:T(8,128)} fusion(f32[3,1024,256]{2,1,0:T(8,128)S(1)} %bitcast.32, f32[1024,1024]{1,0:T(8,128)S(1)} %copy-done), kind=kOutput, calls=%fused_computation.6 | convolution fusion | flops 9664462848 | bytes 10485760 | tf_op jit(solution)/shard_map/wja,ij->awi/dot_general | solution.py:38
  203.3 0.0 reduce-scatter.2.cloned.1.call-update
  203.3 0.2 compare_reduce_fusion
  203.5 0.1 broadcast_bitcast_fusion
  203.6 15.8 %fusion = f32[3,4,256,256]{3,1,2,0:T(4,128)S(1)} fusion(f32[3,16,256,256]{3,2,1,0:T(8,128)} %bitcast.30, s32[3,16]{1,0:T(4,128)S(1)} %select_reduce_fusion, s32[4]{0:T(128)S(1)} %iota_add_fusion), kind=kOutput, calls=%fused_computation | convolution fusion | flops 150995136 | bytes 15728848 | tf_op jit(solution)/shard_map/wsi,wiab->wsab/dot_general | solution.py:32
  219.4 0.5 copy.16
  220.0 0.0 copy-start.2
  220.0 72.0 %reduce-scatter.2.cloned.1.call-done = f32[16,3,1024]{2,0,1:T(8,128)} async-done(((f32[256,3,1024]{2,0,1:T(8,128)}), f32[16,3,1024]{2,0,1:T(8,128)}) %reduce-scatter.2.cloned.1.call-update) | async-done | bytes 196624 | tf_op jit(solution)/shard_map/reduce_scatter | solution.py:37
  292.0 0.9 broadcast_multiply_fusion
  293.0 0.0 copy-start.1
  293.0 1.7 convolution_bitcast_fusion
  294.7 34.8 %all-gather = f32[256,3,256]{2,0,1:T(8,128)S(1)} all-gather(f32[16,3,256]{2,0,1:T(8,128)S(1)} %convolution_bitcast_fusion), channel_id=2, replica_groups=mesh['pole'=2,'prow'=16,'pcol'=16] {'prow'}, dimensions={0}, use_global_device_ids=true | all-gather | bytes 835584 | tf_op jit(solution)/shard_map/all_gather | solution.py:45
  329.6 0.1 reduce_sum.19
  329.6 0.0 copy-done.2
  329.7 0.6 sub.3
  330.3 0.0 copy-done.1
  (4 shorter events, 0.0 us)
Async XLA Ops:
  7.2 155.5 %all-gather.3.cloned.1.call-start = ((), (), s32[]{:S(2)}) async-start(), calls=%async_computation.1 | async-start | bytes 13369344 | tf_op jit(solution)/shard_map/all_gather | solution.py:26
  7.9 284.1 %reduce-scatter.2.cloned.1.call-start = ((), (), s32[]{:S(2)}) async-start(), calls=%async_computation.2 | async-start | bytes 3342336 | tf_op jit(solution)/shard_map/reduce_scatter | solution.py:37
  178.8 2.2 copy-start
  220.0 109.6 %copy-start.2 = (f32[16,3,256]{2,0,1:T(8,128)S(1)}, f32[16,3,256]{2,0,1:T(8,128)}, u32[]{:S(2)}) copy-start(f32[16,3,256]{2,0,1:T(8,128)} %param.7) | copy-start | bytes 147460
  293.0 37.3 %copy-start.1 = (f32[16,3,1024]{2,0,1:T(8,128)}, f32[16,3,1024]{2,0,1:T(8,128)S(1)}, u32[]{:S(2)}) copy-start(f32[16,3,1024]{2,0,1:T(8,128)S(1)} %broadcast_multiply_fusion) | copy-start | bytes 589828
Sparse Core Ops, SparseCore 0:
  10.1 152.5 all-gather.2
  203.4 88.5 reduce-scatter.1

commit v2 on v0

--- a/solution.py
+++ b/solution.py
@@ -23,7 +23,8 @@
     slots = jnp.arange(owned, dtype=jnp.int32)
     col_slots = col_index * owned + slots
     row_slots = row_index * owned + slots
-    piece = lax.all_gather(factor_blocks, "prow", axis=1, tiled=True)
+    stack = jnp.stack([factor_blocks] * lax.axis_size("prow"))
+    piece = jnp.concatenate(lax.all_to_all(stack, "prow", 0, 0), axis=1)
     count = piece.shape[1] // width
     blocks = piece.reshape(window, count, width, width)
     col_pick = (positions[:, None, :] == col_slots[None, :, None]).astype(jnp.float32)

time: 365 us -> 776 us (2.13)
  waiting for transfers between devices: 226 us -> 616 us
  starting transfers between devices: 0.08 us -> 15.4 us
    all_to_all x0 -> x1, waiting for transfers between devices: none -> 542 us  [shards(): piece = jnp.concatenate(lax.all_to_all(stack, 'prow', 0, 0), axis=1)]
    all_gather x1 -> x0, waiting for transfers between devices: 154 us -> none  [shards(): piece = lax.all_gather(factor_blocks, 'prow', axis=1, tiled=True)]
    all_to_all x0 -> x1, starting transfers between devices: none -> 15.4 us  [shards(): piece = jnp.concatenate(lax.all_to_all(stack, 'prow', 0, 0), axis=1)]
  transfers between devices with their start and end apart: 2 -> 2, of which waited for: 2 -> 2; matrix products, arithmetic and copies ran while one was open for 5% -> 2% of each run, Pallas kernels for 0% -> 0%
where the time goes in v2:
time: 776 us; the launch traced here: 770 us
  waiting for transfers between devices  616 us (79%)
  blocking collectives  56.9 us (7%)
  matrix products  56 us (7%)
  starting transfers between devices  15.4 us (2%)
  between operations  14.4 us (2%)
  local copies, waits for them, and re-layouts  9.91 us (1%)
    all_to_all x1, waiting for transfers between devices, shards(): piece = jnp.concatenate(lax.all_to_all(stack, 'prow', 0, 0), axis=1)  542 us
    reduce_scatter x1, waiting for transfers between devices, shards(): lax.psum_scatter(-jnp.einsum('wja,ij->awi', col_factor, inverse_trailing,...  74 us
    psum x1, blocking collectives, shards(): total_diag = lax.psum(local_diag, 'prow')  56.9 us
    dot_general x1, matrix products, shards(): jnp.einsum('wja,ij->awi', col_factor, inverse_trailing, precision=lax.Pre...  22.3 us
    dot_general x1, matrix products, shards(): jnp.einsum('wsi,wiab->wsab', col_pick, blocks, precision=lax.Precision.HI...  16.1 us
    dot_general x1, matrix products, shards(): jnp.einsum('wsi,wiab->wsab', row_pick, blocks, precision=lax.Precision.HI...  15.9 us
  transfers between devices with their start and end apart: 2, of which 2 were waited for; matrix products, arithmetic and copies ran while one was open for 2% of the time, Pallas kernels for 0%

profile of v2, /device:TPU:2, one launch (start us, length us, event | category | flops | bytes accessed | tf_op | source)
XLA Modules:
  0.0 770.1 jit_solution(17285341397212428059)
XLA Ops:
  7.2 7.1 stack.2
  14.3 0.0 copy-start.3
  14.3 0.0 copy-start.4
  14.3 15.4 %all-to-all-start = ((f32[16,3,256,256]{3,2,1,0:T(8,128)}), f32[16,3,256,256]{3,2,1,0:T(8,128)}, u32[]{:S(2)}, u32[]{:S(2)}) async-start(f32[16,3,256,256]{3,2,1,0:T(8,128)} %stack.2), calls=%async_computation | async-start | bytes 25165824 | tf_op jit(solution)/shard_map/all_to_all | solution.py:27
  29.6 0.0 reduce-scatter.2.cloned.1.call-start
  29.7 0.0 copy-done.3
  29.7 0.0 copy-done.4
  29.7 0.2 select_reduce_fusion
  29.9 541.5 %all-to-all-done = f32[16,3,256,256]{3,2,1,0:T(8,128)} async-done(((f32[16,3,256,256]{3,2,1,0:T(8,128)}), f32[16,3,256,256]{3,2,1,0:T(8,128)}, u32[]{:S(2)}, u32[]{:S(2)}) %all-to-all-start) | async-done | bytes 12582944 | tf_op jit(solution)/shard_map/all_to_all | solution.py:27
  571.5 16.1 %fusion.2 = f32[3,4,256,256]{3,1,2,0:T(4,128)S(1)} fusion(f32[16,3,256,256]{3,2,1,0:T(8,128)} %all-to-all-done, s32[3,16]{1,0:T(4,128)S(1)} %select_reduce_fusion, s32[4]{0:T(128)S(1)} %iota_add_fusion.1), kind=kOutput, calls=%fused_computation.2 | convolution fusion | flops 150995136 | bytes 15728848 | tf_op jit(solution)/shard_map/wsi,wiab->wsab/dot_general | solution.py:32
  587.6 0.0 copy-start
  587.6 0.5 copy.15
  588.1 1.6 copy-done
  589.8 22.3 %negate_bitcast_fusion = f32[256,3,1024]{2,0,1:T(8,128)} fusion(f32[3,1024,256]{2,1,0:T(8,128)S(1)} %bitcast.33, f32[1024,1024]{1,0:T(8,128)S(1)} %copy-done), kind=kOutput, calls=%fused_computation.8 | convolution fusion | flops 9664462848 | bytes 10485760 | tf_op jit(solution)/shard_map/wja,ij->awi/dot_general | solution.py:39
  612.1 0.0 reduce-scatter.2.cloned.1.call-update
  612.1 0.2 compare_reduce_fusion
  612.3 0.1 broadcast_bitcast_fusion
  612.4 15.9 %fusion = f32[3,4,256,256]{3,1,2,0:T(4,128)S(1)} fusion(f32[16,3,256,256]{3,2,1,0:T(8,128)} %all-to-all-done, s32[3,16]{1,0:T(4,128)S(1)} %select_reduce_fusion, s32[4]{0:T(128)S(1)} %iota_add_fusion), kind=kOutput, calls=%fused_computation | convolution fusion | flops 150995136 | bytes 15728848 | tf_op jit(solution)/shard_map/wsi,wiab->wsab/dot_general | solution.py:33
  628.3 0.5 copy.17
  628.8 0.0 copy-start.2
  628.8 74.0 %reduce-scatter.2.cloned.1.call-done = f32[16,3,1024]{2,0,1:T(8,128)} async-done(((f32[256,3,1024]{2,0,1:T(8,128)}), f32[16,3,1024]{2,0,1:T(8,128)}) %reduce-scatter.2.cloned.1.call-update) | async-done | bytes 196624 | tf_op jit(solution)/shard_map/reduce_scatter | solution.py:38
  702.8 0.9 broadcast_multiply_fusion
  703.8 0.0 copy-start.1
  703.8 1.7 convolution_bitcast_fusion
  705.5 56.9 %psum.7 = f32[16,3,256]{2,0,1:T(8,128)S(1)} all-reduce(f32[16,3,256]{2,0,1:T(8,128)S(1)} %convolution_bitcast_fusion), channel_id=1, replica_groups=mesh['pole'=2,'prow'=16,'pcol'=16] {'prow'}, use_global_device_ids=true, to_apply=%region_3.4 | all-reduce | flops 12288 | bytes 98304 | tf_op jit(solution)/shard_map/psum | solution.py:46
  762.4 0.0 copy-done.2
  762.4 0.6 sub.3
  763.0 0.0 copy-done.1
  (4 shorter events, 0.0 us)
Async XLA Ops:
  14.3 15.5 %copy-start.3 = (s32[3,16]{1,0:T(4,128)S(1)}, s32[3,16]{1,0:T(4,128)}, u32[]{:S(2)}) copy-start(s32[3,16]{1,0:T(4,128)} %param.8) | copy-start | bytes 580
  14.3 15.5 %copy-start.4 = (s32[64]{0:T(128)S(1)}, s32[64]{0:T(128)}, u32[]{:S(2)}) copy-start(s32[64]{0:T(128)} %param.9) | copy-start | bytes 772
  14.3 557.2 %all-to-all-start = ((f32[16,3,256,256]{3,2,1,0:T(8,128)}), f32[16,3,256,256]{3,2,1,0:T(8,128)}, u32[]{:S(2)}, u32[]{:S(2)}) async-start(f32[16,3,256,256]{3,2,1,0:T(8,128)} %stack.2), calls=%async_computation | async-start | bytes 25165824 | tf_op jit(solution)/shard_map/all_to_all | solution.py:27
  29.6 673.2 %reduce-scatter.2.cloned.1.call-start = ((), (), s32[]{:S(2)}) async-start(), calls=%async_computation.2 | async-start | bytes 3342336 | tf_op jit(solution)/shard_map/reduce_scatter | solution.py:38
  587.6 2.2 copy-start
  628.8 133.6 %copy-start.2 = (f32[16,3,256]{2,0,1:T(8,128)S(1)}, f32[16,3,256]{2,0,1:T(8,128)}, u32[]{:S(2)}) copy-start(f32[16,3,256]{2,0,1:T(8,128)} %param.7) | copy-start | bytes 147460
  703.8 59.3 %copy-start.1 = (f32[16,3,1024]{2,0,1:T(8,128)}, f32[16,3,1024]{2,0,1:T(8,128)S(1)}, u32[]{:S(2)}) copy-start(f32[16,3,1024]{2,0,1:T(8,128)S(1)} %broadcast_multiply_fusion) | copy-start | bytes 589828
Sparse Core Ops, SparseCore 0:
  612.2 90.5 reduce-scatter.1
